TPU v7x, 32 devices: a whole 2x2x4 slice. The times are simulated.
32 devices in a mesh: req: 16 (over z, x, core), ep: 2 (over y).
Axes of the slice: x: 2, y: 2, z: 4, core: 2. Of those that a mesh axis runs over, the one named last changes fastest.
Arguments:
- hidden: bfloat16 [16, 512, 1536], P('req', None, 'ep'), may hold values from -6 to 6
- key_cache: bfloat16 [16, 8, 2560, 64], P('req', 'ep'), may hold values from -160 to 160
- value_cache: bfloat16 [16, 8, 2560, 64], P('req', 'ep'), may hold values from -6 to 6
- request_order: int32 [16], replicated, may hold values from 0 to 15, each once
- cached_lengths: int32 [16], replicated, may hold values from 1 to 2048, 16384 in all
- expert_ids: int32 [16, 512, 8], P('req'), may hold values from 0 to 39, all different within a row; in each aligned block of 512 rows (0 to 511, 512 to 1023, ..., all dimensions but the last counted through in order) at most 192 rows name the same one
- gate_values: float32 [16, 512, 8], P('req'), may hold values from 0.1 to 1
- attn_gain: float32 [1536], replicated, may hold values from 0.25 to 1.75
- ffn_gain: float32 [1536], replicated, may hold values from 0.25 to 1.75
- w_query: bfloat16 [1536, 1536], P(None, 'ep'), may hold values from -0.15625 to 0.15625
- w_key: bfloat16 [1536, 512], P(None, 'ep'), may hold values from -0.15625 to 0.15625
- w_value: bfloat16 [1536, 512], P(None, 'ep'), may hold values from -0.15625 to 0.15625
- w_out: bfloat16 [1536, 1536], P('ep'), may hold values from -0.15625 to 0.15625
- expert_gate: bfloat16 [4, 1536, 512], P('ep', 'req'), may hold values from -0.15625 to 0.15625
- expert_up: bfloat16 [4, 1536, 512], P('ep', 'req'), may hold values from -0.15625 to 0.15625
- expert_down: bfloat16 [4, 512, 1536], P('ep', 'req'), may hold values from -0.25 to 0.25
Outputs:
- hidden_out: bfloat16 [16, 512, 1536], P('req', None, 'ep')
- key_cache_out: bfloat16 [16, 8, 2560, 64], P('req', 'ep')
- value_cache_out: bfloat16 [16, 8, 2560, 64], P('req', 'ep')
Inputs may be any that keep to these rules, and one draw needn't show every extreme that they name: Slot s holds request request_order[s]; every request is held by one slot. `cached_lengths`: the longest cached length is exactly 2048. `expert_ids`: each token names 8 different experts; among the 512 tokens of one slot no expert is named by more than 192 tokens, a bound that some block reaches.
All inputs are finite; a program needn't handle non-finite values.
Results may differ from a plain program's by a relative error of at most 0.012.
The roundings to bfloat16 on the way count: a program that leaves them out, or rounds other values in their place, can miss the bound.
Values may be sent and summed in bfloat16 or wider, within the bound.
No kernel may reach another device: no remote copies, remote signals or barrier semaphores. Data moves between devices by JAX's collectives and lax.ppermute only.
A program may use at most 128 MiB of HBM per device.

v0:
```python
import jax
import jax.numpy as jnp
from jax import lax
from jax.experimental import pallas as pl
from jax.experimental.pallas import tpu as pltpu
from jax.sharding import PartitionSpec as P

epsilon = 1e-06


def normalize(values, gain):
    return values * lax.rsqrt(jnp.mean(values * values, -1, keepdims=True) + epsilon) * gain


def rotate(values, positions):
    half = values.shape[-1] // 2
    freq = 10000.0 ** (-jnp.arange(half, dtype=jnp.float32) * (2.0 / values.shape[-1]))
    angle = positions.astype(jnp.float32)[:, None] * freq[None, :]
    cosine = jnp.cos(angle)
    sine = jnp.sin(angle)
    first = values[..., :half]
    second = values[..., half:]
    return jnp.concatenate([first * cosine - second * sine, second * cosine + first * sine], -1)


def rounded(values):
    return lax.optimization_barrier(values.astype(jnp.bfloat16)).astype(jnp.float32)


def route_tables(chosen, gate_rows, wanted, capacity):
    hits = chosen[:, :, None] == wanted[None, None, :]
    member = jnp.sum(hits.astype(jnp.int32), 1, dtype=jnp.int32)
    weight = jnp.sum(jnp.where(hits, gate_rows[:, :, None], 0.0), 1)
    place = jnp.cumsum(member, 0, dtype=jnp.int32) - 1
    slots = jnp.arange(capacity, dtype=jnp.int32)
    table = (member.T[:, None, :] == 1) & (place.T[:, None, :] == slots[None, :, None])
    gate_slot = jnp.sum(jnp.where(table, weight.T[:, None, :], 0.0), 2)
    return (table.astype(jnp.bfloat16), gate_slot)


def flash_attend(query, keys, values, length, new_rows):
    kv_heads, rows, head_dim = query.shape
    block = new_rows
    blocks = keys.shape[1] // block
    limit = (length + jnp.arange(rows, dtype=jnp.int32) % new_rows)[:, None]

    def last_block(length_ref):
        return (length_ref[0] + new_rows - 1) // block

    def kernel(length_ref, limit_ref, q_ref, k_ref, v_ref, o_ref, m_sc, l_sc, acc_sc):
        step = pl.program_id(1)

        @pl.when(step == 0)
        def _():
            m_sc[...] = jnp.full(m_sc.shape, -1e30, jnp.float32)
            l_sc[...] = jnp.zeros(l_sc.shape, jnp.float32)
            acc_sc[...] = jnp.zeros(acc_sc.shape, jnp.float32)

        def visit(masked):
            scores = lax.dot_general(
                q_ref[0],
                k_ref[0],
                (((1,), (1,)), ((), ())),
                preferred_element_type=jnp.float32,
            )
            if masked:
                column = step * block + lax.broadcasted_iota(jnp.int32, scores.shape, 1)
                visible = column <= limit_ref[...]
                scores = jnp.where(visible, scores, -1e30)
            previous = m_sc[...]
            highest = jnp.maximum(previous, jnp.max(scores, -1, keepdims=True))
            probs = jnp.exp(scores - highest)
            if masked:
                probs = jnp.where(visible, probs, 0.0)
            correction = jnp.exp(previous - highest)
            l_sc[...] = l_sc[...] * correction + jnp.sum(probs, -1, keepdims=True)
            acc_sc[...] = acc_sc[...] * correction + jnp.dot(
                probs.astype(jnp.bfloat16), v_ref[0], preferred_element_type=jnp.float32
            )
            m_sc[...] = highest

        whole = (step + 1) * block - 1 <= length_ref[0]

        @pl.when(whole)
        def _():
            visit(False)

        @pl.when(jnp.logical_not(whole) & (step <= last_block(length_ref)))
        def _():
            visit(True)

        @pl.when(step == blocks - 1)
        def _():
            o_ref[0] = (acc_sc[...] / l_sc[...]).astype(o_ref.dtype)

    def kv_map(head, step, length_ref):
        return (head, jnp.minimum(step, last_block(length_ref)), 0)

    grid_spec = pltpu.PrefetchScalarGridSpec(
        num_scalar_prefetch=1,
        grid=(kv_heads, blocks),
        in_specs=[
            pl.BlockSpec((rows, 1), lambda head, step, length_ref: (0, 0)),
            pl.BlockSpec((1, rows, head_dim), lambda head, step, length_ref: (head, 0, 0)),
            pl.BlockSpec((1, block, head_dim), kv_map),
            pl.BlockSpec((1, block, head_dim), kv_map),
        ],
        out_specs=pl.BlockSpec((1, rows, head_dim), lambda head, step, length_ref: (head, 0, 0)),
        scratch_shapes=[
            pltpu.VMEM((rows, 1), jnp.float32),
            pltpu.VMEM((rows, 1), jnp.float32),
            pltpu.VMEM((rows, head_dim), jnp.float32),
        ],
    )
    flops = 4 * kv_heads * rows * keys.shape[1] * head_dim
    return pl.pallas_call(
        kernel,
        grid_spec=grid_spec,
        out_shape=jax.ShapeDtypeStruct(query.shape, jnp.bfloat16),
        compiler_params=pltpu.CompilerParams(dimension_semantics=("arbitrary", "arbitrary")),
        cost_estimate=pl.CostEstimate(
            flops=flops,
            transcendentals=kv_heads * rows * keys.shape[1],
            bytes_accessed=2 * (query.size + keys.size + values.size + query.size),
        ),
    )(length.reshape(1), limit, query, keys, values)


def shifted(values, shift):
    devices = lax.axis_size("ep")
    return lax.ppermute(values, "ep", [(i, (i + shift) % devices) for i in range(devices)])


def gather_columns(values):
    devices = lax.axis_size("ep")
    me = lax.axis_index("ep")
    width = values.shape[-1]
    whole = jnp.zeros(values.shape[:-1] + (width * devices,), values.dtype)
    for shift in range(devices):
        piece = values if shift == 0 else shifted(values, shift)
        source = (me - shift) % devices
        whole = lax.dynamic_update_slice_in_dim(whole, piece, source * width, values.ndim - 1)
    return whole


def sum_over_ep(part):
    devices = lax.axis_size("ep")
    half = part.shape[0] // 2
    total = part.astype(jnp.float32)
    for shift in range(1, devices):
        upper = shifted(part[:half], shift)
        lower = shifted(part[half:], shift)
        total = total + jnp.concatenate([upper, lower], 0).astype(jnp.float32)
    return total


def scatter_sum_over_ep(part, width):
    devices = lax.axis_size("ep")
    me = lax.axis_index("ep")
    total = lax.dynamic_slice_in_dim(part, me * width, width, 1).astype(jnp.float32)
    for shift in range(1, devices):
        target = (me + shift) % devices
        piece = lax.dynamic_slice_in_dim(part, target * width, width, 1)
        total = total + shifted(piece, shift).astype(jnp.float32)
    return total


def on_device(
    hidden,
    key_cache,
    value_cache,
    request_order,
    cached_lengths,
    expert_ids,
    gate_values,
    attn_gain,
    ffn_gain,
    w_query,
    w_key,
    w_value,
    w_out,
    expert_gate,
    expert_up,
    expert_down,
):
    own_rows = hidden[0]
    new_rows = own_rows.shape[0]
    own_width = own_rows.shape[1]
    head_dim = key_cache.shape[3]
    kv_local = key_cache.shape[1]
    heads_local = w_query.shape[1] // head_dim
    group = heads_local // kv_local
    per_device = expert_gate.shape[0]
    capacity = 3 * new_rows // 8
    me = lax.axis_index("ep")
    gate_whole = lax.all_gather(expert_gate, "req", axis=1, tiled=True)
    up_whole = lax.all_gather(expert_up, "req", axis=1, tiled=True)
    down_whole = lax.all_gather(expert_down, "req", axis=1, tiled=True)
    everyone = jnp.arange(request_order.shape[0], dtype=jnp.int32)
    request = jnp.sum(jnp.where(everyone == lax.axis_index("req"), request_order, 0))
    length = jnp.sum(jnp.where(everyone == request, cached_lengths, 0))
    rows_whole = gather_columns(own_rows)
    rows_f = rows_whole.astype(jnp.float32)
    normed = normalize(rows_f, attn_gain).astype(jnp.bfloat16)
    query = jnp.dot(normed, w_query, preferred_element_type=jnp.float32)
    key_new = jnp.dot(normed, w_key, preferred_element_type=jnp.float32)
    value_new = jnp.dot(normed, w_value, preferred_element_type=jnp.float32)
    positions = length + jnp.arange(new_rows, dtype=jnp.int32)
    query = rotate(
        query.reshape(new_rows, heads_local, head_dim).transpose(1, 0, 2), positions
    ).astype(jnp.bfloat16) * jnp.asarray(head_dim ** (-0.5), jnp.bfloat16)
    query = query.reshape(kv_local, group * new_rows, head_dim)
    key_new = rotate(
        key_new.reshape(new_rows, kv_local, head_dim).transpose(1, 0, 2), positions
    ).astype(jnp.bfloat16)
    value_new = (
        value_new.reshape(new_rows, kv_local, head_dim).transpose(1, 0, 2).astype(jnp.bfloat16)
    )
    zero = jnp.zeros((), jnp.int32)
    keys = lax.dynamic_update_slice(key_cache[0], key_new, (zero, length, zero))
    values = lax.dynamic_update_slice(value_cache[0], value_new, (zero, length, zero))
    attended = flash_attend(query, keys, values, length, new_rows)
    attended = (
        attended.reshape(heads_local, new_rows, head_dim)
        .transpose(1, 0, 2)
        .reshape(new_rows, heads_local * head_dim)
    )
    head_part = jnp.dot(attended, w_out, preferred_element_type=jnp.float32).astype(jnp.bfloat16)
    head_sum = sum_over_ep(head_part)
    mixed_f = (rows_f + head_sum).astype(jnp.bfloat16).astype(jnp.float32)
    ffn_normed = normalize(mixed_f, ffn_gain).astype(jnp.bfloat16)
    table, gate_slot = route_tables(
        expert_ids[0],
        gate_values[0],
        me * per_device + jnp.arange(per_device, dtype=jnp.int32),
        capacity,
    )
    dispatched = jnp.einsum(
        "ect,td->ecd", table, ffn_normed, preferred_element_type=jnp.float32
    ).astype(jnp.bfloat16)
    gate_whole, up_whole, down_whole, dispatched = lax.optimization_barrier(
        (gate_whole, up_whole, down_whole, dispatched)
    )
    gate_act = jnp.einsum("ecd,edf->ecf", dispatched, gate_whole, preferred_element_type=jnp.float32)
    up_act = jnp.einsum("ecd,edf->ecf", dispatched, up_whole, preferred_element_type=jnp.float32)
    act = (jax.nn.silu(gate_act) * up_act).astype(jnp.bfloat16)
    output = jnp.einsum("ecf,efd->ecd", act, down_whole, preferred_element_type=jnp.float32)
    contrib = (output * gate_slot[..., None]).astype(jnp.bfloat16)
    expert_part = jnp.einsum(
        "ect,ecd->td", table, contrib, preferred_element_type=jnp.float32
    ).astype(jnp.bfloat16)
    expert_sum = scatter_sum_over_ep(expert_part, own_width)
    mixed_own = lax.dynamic_slice_in_dim(mixed_f, me * own_width, own_width, 1)
    result = (mixed_own + expert_sum).astype(jnp.bfloat16)
    return (result[None], keys[None], values[None])


def solution(mesh):
    in_specs = (
        P("req", None, "ep"),
        P("req", "ep", None, None),
        P("req", "ep", None, None),
        P(),
        P(),
        P("req", None, None),
        P("req", None, None),
        P(),
        P(),
        P(None, "ep"),
        P(None, "ep"),
        P(None, "ep"),
        P("ep", None),
        P("ep", "req", None),
        P("ep", "req", None),
        P("ep", "req", None),
    )
    out_specs = (P("req", None, "ep"), P("req", "ep", None, None), P("req", "ep", None, None))
    return jax.shard_map(
        on_device, mesh=mesh, in_specs=in_specs, out_specs=out_specs, check_vma=False
    )
```

profile of v0, /device:TPU:18, one launch (start us, length us, event | category | flops | bytes accessed | tf_op | source)
XLA Modules:
  0.0 230.6 jit_solution(1413296551051774150)
XLA Ops:
  7.2 0.0 all-gather.4.cloned.1.call-start
  7.2 0.7 all-gather.4.cloned.1.call-update
  7.9 0.0 all-gather.6.cloned.1.call-start
  8.0 0.7 all-gather.6.cloned.1.call-update
  8.7 0.0 all-gather.8.cloned.1.call-start
  8.7 1.6 collective-permute-start
  10.3 0.0 all-gather.8.cloned.1.call-update
  10.3 1.3 fusion.26
  11.6 2.0 fusion.27
  13.7 0.7 add_convert_fusion.3
  14.4 0.3 multiply_cosine_fusion
  15.4 0.8 copy.57
  16.2 0.8 copy.58
  17.8 3.8 %copy.55 = bf16[1,4,2560,64]{3,2,1,0:T(8,128)(2,1)} copy(bf16[1,4,2560,64]{2,3,1,0:T(8,128)(2,1)} %param.17) | data formatting | bytes 2621440 | tf_op args[1]
  21.6 3.9 %copy.59 = bf16[1,4,2560,64]{3,2,1,0:T(8,128)(2,1)} copy(bf16[1,4,2560,64]{2,3,1,0:T(8,128)(2,1)} %param.18) | data formatting | bytes 2621440 | tf_op args[2]
  25.6 1.6 fusion.12.limit_ref
  27.2 0.1 fusion.24
  27.3 1.2 reduce-window.6
  29.2 0.1 broadcast_in_dim.35
  29.4 0.1 constant_dynamic-update-slice_fusion.1
  29.5 1.3 constant_dynamic-update-slice_fusion
  30.7 0.4 fusion
  31.1 1.6 fusion.29
  32.7 1.4 copy.56
  34.1 3.1 %convolution_convert_fusion.2 = bf16[512,256]{0,1:T(8,128)(2,1)} fusion(bf16[1536,256]{1,0:T(8,128)(2,1)} %param.27, bf16[512,1536]{1,0:T(8,128)(2,1)} %copy-done.2, f32[1536]{0:T(1024)} %param.23, f32[512]{0:T(512)} %copy-done.16), kind=kOutput, calls=%fused_computation.23 | convolution fusion | flops 405929984 | bytes 2629632 | tf_op jit(solution)/shard_map/dot_general | solution.py:207
  37.2 2.0 copy.60
  39.2 3.7 %fusion.31 = f32[512,768]{0,1:T(8,128)S(1)} fusion(bf16[1536,768]{1,0:T(8,128)(2,1)} %param.25, bf16[512,1536]{1,0:T(8,128)(2,1)} %copy-done.2, f32[1536]{0:T(1024)} %param.23, f32[512]{0:T(512)} %copy-done.16), kind=kOutput, calls=%fused_computation.66 | convolution fusion | flops 1211105280 | bytes 5513216 | tf_op jit(solution)/shard_map/dot_general | solution.py:205
  42.9 1.2 subtract_convert_fusion.1
  44.1 2.4 %copy.53 = bf16[12,512,32]{2,1,0:T(8,128)(2,1)} copy(bf16[12,512,32]{1,2,0:T(8,128)(2,1)} %get-tuple-element.25) | data formatting | bytes 786432 | tf_op jit(solution)/shard_map/convert.5
  46.5 2.4 %copy.54 = bf16[12,512,32]{2,1,0:T(8,128)(2,1)} copy(bf16[12,512,32]{1,2,0:T(8,128)(2,1)} %get-tuple-element.26) | data formatting | bytes 786432 | tf_op jit(solution)/shard_map/convert.4
  48.9 1.5 subtract_convert_fusion
  50.4 0.3 pad_maximum_fusion
  50.7 5.0 %dynamic_update_slice.14.k_ref = bf16[4,2560,64]{2,1,0:T(8,128)(2,1)} dynamic-update-slice(bf16[4,2560,64]{2,1,0:T(8,128)(2,1)} %bitcast.53, bf16[4,512,64]{2,1,0:T(8,128)(2,1)S(1)} %pad_maximum_fusion, s32[]{:T(128)} %constant.61.clone.1, s32[]{:T(128)S(6)} %select_n.67, s32[]{:T(128)} %constant.61.clone.1) | dynamic-update-slice | bytes 524292 | tf_op jit(solution)/shard_map/dynamic_update_slice | solution.py:220
  55.6 4.9 %dynamic_update_slice.15.v_ref = bf16[4,2560,64]{2,1,0:T(8,128)(2,1)} dynamic-update-slice(bf16[4,2560,64]{2,1,0:T(8,128)(2,1)} %bitcast.51, bf16[4,512,64]{2,1,0:T(8,128)(2,1)S(1)} %bitcast.59, s32[]{:T(128)} %constant.61.clone.1, s32[]{:T(128)S(6)} %select_n.67, s32[]{:T(128)} %constant.61.clone.1) | dynamic-update-slice | bytes 524292 | tf_op jit(solution)/shard_map/dynamic_update_slice | solution.py:221
  60.6 4.0 %maximum_multiply_fusion.q_ref = bf16[4,1536,64]{2,1,0:T(8,128)(2,1)} fusion(bf16[4,1536,32]{2,1,0:T(8,128)(2,1)} %bitcast.57, bf16[4,1536,32]{2,1,0:T(8,128)(2,1)} %bitcast.56), kind=kLoop, calls=%fused_computation.17 | loop fusion | flops 2359296 | bytes 1572864 | tf_op jit(solution)/shard_map/mul | solution.py:209
  64.6 80.0 %shard_map.175 = bf16[4,1536,64]{2,1,0:T(8,128)(2,1)} custom-call(s32[1]{0:T(128)} %bitcast.1.length_ref, s32[1536,1]{1,0:T(8,128)} %fusion.12.limit_ref, bf16[4,1536,64]{2,1,0:T(8,128)(2,1)} %maximum_multiply_fusion.q_ref, bf16[4,2560,64]{2,1,0:T(8,128)(2,1)} %dynamic_update_slice.14.k_ref, bf16[4,2560,64]{2,1,0:T(8,128)(2,1)} %dynamic_update_slice.15.v_ref), custom_call_target="tpu_custom_call" | custom-call | flops 4026531840 | bytes 4194304 | tf_op jit(solution)/shard_map/pallas_call | solution.py:116
  144.6 1.9 copy.61
  146.5 1.4 convolution_convert_fusion
  148.0 1.2 copy-done.3
  149.1 1.2 fusion.34
  150.4 0.5 collective-permute-start.1
  150.9 1.5 collective-permute-start.2
  152.4 0.2 slice_reduce_fusion
  152.6 0.2 reduce-window.9
  152.8 0.1 add_bitcast_fusion
  152.9 0.1 fusion.25
  153.0 0.2 select_reduce_fusion
  153.2 17.8 %collective-permute-done.1 = bf16[256,1536]{1,0:T(8,128)(2,1)S(1)} collective-permute-done((bf16[256,1536]{1,0:T(8,128)(2,1)}, bf16[256,1536]{1,0:T(8,128)(2,1)S(1)}, u32[]{:S(2)}, u32[]{:S(2)}) %collective-permute-start.1) | collective-permute-done | bytes 786464 | tf_op jit(solution)/shard_map/ppermute | solution.py:131
  171.1 15.4 %collective-permute-done.2 = bf16[256,1536]{1,0:T(8,128)(2,1)} collective-permute-done((bf16[256,1536]{1,0:T(8,128)(2,1)}, bf16[256,1536]{1,0:T(8,128)(2,1)}, u32[]{:S(2)}, u32[]{:S(2)}) %collective-permute-start.2) | collective-permute-done | bytes 786464 | tf_op jit(solution)/shard_map/ppermute | solution.py:131
  186.4 2.9 %multiply_reduce_fusion = (f32[512]{0:T(512)S(1)}, f32[512,1536]{1,0:T(8,128)S(1)}) fusion(bf16[256,1536]{1,0:T(8,128)(2,1)} %collective-permute-done.2, bf16[256,1536]{1,0:T(8,128)(2,1)S(1)} %collective-permute-done.1, bf16[512,1536]{1,0:T(8,128)(2,1)} %copy-done.3, bf16[512,1536]{1,0:T(8,128)(2,1)} %copy-done.2), kind=kLoop, calls=%fused_computation.9 | loop fusion | flops 9436672 | bytes 7866368 | tf_op jit(solution)/shard_map/reduce_sum | solution.py:12
  189.3 1.6 copy-done.1
  191.0 1.6 convolution_convert_fusion.1
  192.6 0.0 all-gather.4.cloned.1.call-done
  192.6 0.0 all-gather.6.cloned.1.call-done
  192.6 0.0 all-gather.8.cloned.1.call-done
  192.7 2.8 %fusion.35 = f32[2,192,512]{2,1,0:T(8,128)S(1)} fusion(bf16[2,192,1536]{2,1,0:T(8,128)(2,1)S(1)} %convolution_convert_fusion.1, bf16[2,1536,512]{2,1,0:T(8,128)(2,1)} %all-gather.4.cloned.1.call-done), kind=kOutput, calls=%fused_computation.68 | convolution fusion | flops 603979776 | bytes 5111808 | tf_op jit(solution)/shard_map/ecd,edf->ecf/dot_general | solution.py:244
  195.5 1.6 fusion.11
  197.1 4.8 %fusion.4 = bf16[512,1536]{1,0:T(8,128)(2,1)} fusion(bf16[2,192,512]{2,1,0:T(8,128)(2,1)} %fusion.11, bf16[2,512,1536]{2,1,0:T(8,128)(2,1)} %all-gather.8.cloned.1.call-done, f32[2,192]{1,0:T(2,128)S(1)} %select_reduce_fusion, s32[2,512]{1,0:T(2,128)S(1)} %bitcast.70, pred[2,512]{1,0:T(4,128)(4,1)S(1)} %broadcast_compare_fusion), kind=kOutput, calls=%fused_computation.11 | convolution fusion | flops 1210318848 | bytes 5118464 | tf_op jit(solution)/shard_map/ect,ecd->td/dot_general | solution.py:249
  201.8 1.2 constant_dynamic-slice_fusion
  203.0 1.0 collective-permute-start.3
  204.0 4.0 %copy.62 = bf16[1,4,2560,64]{2,3,1,0:T(8,128)(2,1)} copy(bf16[1,4,2560,64]{3,2,1,0:T(8,128)(2,1)} %bitcast.54) | data formatting | bytes 2621440
  208.0 4.0 %copy.63 = bf16[1,4,2560,64]{2,3,1,0:T(8,128)(2,1)} copy(bf16[1,4,2560,64]{3,2,1,0:T(8,128)(2,1)} %bitcast.52) | data formatting | bytes 2621440
  212.0 9.2 %collective-permute-done.3 = bf16[512,768]{1,0:T(8,128)(2,1)} collective-permute-done((bf16[512,768]{1,0:T(8,128)(2,1)S(1)}, bf16[512,768]{1,0:T(8,128)(2,1)}, u32[]{:S(2)}, u32[]{:S(2)}) %collective-permute-start.3) | collective-permute-done | bytes 786464 | tf_op jit(solution)/shard_map/ppermute | solution.py:131
  221.2 3.0 %fusion.13 = bf16[1,512,768]{2,1,0:T(8,128)(2,1)} fusion(bf16[512,768]{1,0:T(8,128)(2,1)} %collective-permute-done.3, f32[512,1536]{1,0:T(8,128)} %copy-done.1, s32[]{:T(128)S(6)} %select_n.68, bf16[512,1536]{1,0:T(8,128)(2,1)} %fusion.4), kind=kLoop, calls=%fused_computation.28 | loop fusion | flops 1966080 | bytes 3932164 | tf_op jit(solution)/shard_map/broadcast_in_dim | solution.py:255
  (46 shorter events, 0.2 us)
Async XLA Ops:
  7.2 139.4 %copy-start = (bf16[768,1536]{1,0:T(8,128)(2,1)S(1)}, bf16[768,1536]{1,0:T(8,128)(2,1)}, u32[]{:S(2)}) copy-start(bf16[768,1536]{1,0:T(8,128)(2,1)} %param.28) | copy-start | bytes 7077892
  7.2 185.4 %all-gather.4.cloned.1.call-start = ((), (), s32[]{:S(2)}) async-start(), calls=%async_computation | async-start | bytes 3342336 | tf_op jit(solution)/shard_map/all_gather | solution.py:196
  7.9 184.7 %all-gather.6.cloned.1.call-start = ((), (), s32[]{:S(2)}) async-start(), calls=%async_computation.1 | async-start | bytes 3342336 | tf_op jit(solution)/shard_map/all_gather | solution.py:197
  8.7 184.0 %all-gather.8.cloned.1.call-start = ((), (), s32[]{:S(2)}) async-start(), calls=%async_computation.2 | async-start | bytes 3342336 | tf_op jit(solution)/shard_map/all_gather | solution.py:198
  8.7 20.7 %collective-permute-start = (bf16[512,768]{1,0:T(8,128)(2,1)}, bf16[512,768]{1,0:T(8,128)(2,1)}, u32[]{:S(2)}, u32[]{:S(2)}) collective-permute-start(bf16[512,768]{1,0:T(8,128)(2,1)} %bitcast.62), channel_id=1, source_target_pairs={{0,1},{1,0},{2,3},{3,2},{4,5},{5,4},{6,7},{7,6},{8,9},{9,8},{10,11... | collective-permute-start | bytes 2359304 | tf_op jit(solution)/shard_map/ppermute | solution.py:131
  21.6 5.6 %copy-start.6 = (s32[1,512,8]{1,2,0:T(8,128)S(1)}, s32[1,512,8]{1,2,0:T(8,128)}, u32[]{:S(2)}) copy-start(s32[1,512,8]{1,2,0:T(8,128)} %param.21) | copy-start | bytes 49156
  21.6 7.7 %copy-start.5 = (bf16[1,512,768]{2,1,0:T(8,128)(2,1)S(1)}, bf16[1,512,768]{2,1,0:T(8,128)(2,1)}, u32[]{:S(2)}) copy-start(bf16[1,512,768]{2,1,0:T(8,128)(2,1)} %param.16) | copy-start | bytes 2359300
  25.6 1.7 copy-start.14
  27.3 3.4 %copy-start.8 = (s32[512,2]{0,1:T(2,128)}, s32[512,2]{0,1:T(2,128)S(1)}, u32[]{:S(2)}) copy-start(s32[512,2]{0,1:T(2,128)S(1)} %fusion.24) | copy-start | bytes 12292
  29.3 1.8 copy-start.18
  29.4 1.8 copy-start.19
  30.7 2.0 copy-start.2
  31.1 1.6 copy-start.16
  50.4 5.3 %copy-start.4 = (bf16[512,4,64]{2,0,1:T(8,128)(2,1)S(1)}, bf16[512,4,64]{2,0,1:T(8,128)(2,1)}, u32[]{:S(2)}) copy-start(bf16[512,4,64]{2,0,1:T(8,128)(2,1)} %copy.60) | copy-start | bytes 786436
  147.9 1.2 copy-start.3
  149.1 3.3 %copy-start.7 = (s32[2,4,128]{2,1,0:T(4,128)S(1)}, s32[2,4,128]{2,1,0:T(4,128)}, u32[]{:S(2)}) copy-start(s32[2,4,128]{2,1,0:T(4,128)} %reduce-window.6) | copy-start | bytes 12292
  149.1 3.8 %copy-start.12 = (f32[1,512,8]{1,2,0:T(8,128)S(1)}, f32[1,512,8]{1,2,0:T(8,128)}, u32[]{:S(2)}) copy-start(f32[1,512,8]{1,2,0:T(8,128)} %param.22) | copy-start | bytes 49156
  149.1 3.8 %copy-start.15 = (s32[2]{0:T(128)S(1)}, s32[2]{0:T(128)}, u32[]{:S(2)}) copy-start(s32[2]{0:T(128)} %copy-done.14) | copy-start | bytes 28
  149.1 3.9 %copy-start.9 = (s32[512,2]{0,1:T(2,128)S(1)}, s32[512,2]{0,1:T(2,128)}, u32[]{:S(2)}) copy-start(s32[512,2]{0,1:T(2,128)} %copy-done.8) | copy-start | bytes 12292
  150.4 20.7 %collective-permute-start.1 = (bf16[256,1536]{1,0:T(8,128)(2,1)}, bf16[256,1536]{1,0:T(8,128)(2,1)S(1)}, u32[]{:S(2)}, u32[]{:S(2)}) collective-permute-start(bf16[256,1536]{1,0:T(8,128)(2,1)} %get-tuple-element.27), channel_id=1, source_target_pairs={{0,1},{1,0},{2,3},{3,2},{4,5},{5,4},{6,7},{7,6},{8,9},{9,8},{10,11... | collective-permute-start | bytes 2359304 | tf_op jit(solution)/shard_map/ppermute | solution.py:131
  150.9 35.5 %collective-permute-start.2 = (bf16[256,1536]{1,0:T(8,128)(2,1)}, bf16[256,1536]{1,0:T(8,128)(2,1)}, u32[]{:S(2)}, u32[]{:S(2)}) collective-permute-start(bf16[256,1536]{1,0:T(8,128)(2,1)} %get-tuple-element.28), channel_id=1, source_target_pairs={{0,1},{1,0},{2,3},{3,2},{4,5},{5,4},{6,7},{7,6},{8,9},{9,8},{10,11... | collective-permute-start | bytes 2359304 | tf_op jit(solution)/shard_map/ppermute | solution.py:131
  152.9 36.4 %copy-start.10 = (s32[1,2,4,128]{3,1,2,0:T(2,128)}, s32[1,2,4,128]{3,1,2,0:T(2,128)S(1)}, u32[]{:S(2)}) copy-start(s32[1,2,4,128]{3,1,2,0:T(2,128)S(1)} %copy.67) | copy-start | bytes 12292
  153.2 37.7 %copy-start.13 = (f32[1536]{0:T(1024)S(1)}, f32[1536]{0:T(1024)}, u32[]{:S(2)}) copy-start(f32[1536]{0:T(1024)} %param.24) | copy-start | bytes 18436
  189.3 1.6 copy-start.1
  192.7 2.8 %copy-start.17 = (bf16[2,1536,512]{2,1,0:T(8,128)(2,1)S(1)}, bf16[2,1536,512]{2,1,0:T(8,128)(2,1)}, u32[]{:S(2)}) copy-start(bf16[2,1536,512]{2,1,0:T(8,128)(2,1)} %all-gather.6.cloned.1.call-done) | copy-start | bytes 9437188
  195.5 1.6 copy-start.11
  203.0 18.1 %collective-permute-start.3 = (bf16[512,768]{1,0:T(8,128)(2,1)S(1)}, bf16[512,768]{1,0:T(8,128)(2,1)}, u32[]{:S(2)}, u32[]{:S(2)}) collective-permute-start(bf16[512,768]{1,0:T(8,128)(2,1)S(1)} %constant_dynamic-slice_fusion), channel_id=1, source_target_pairs={{0,1},{1,0},{2,3},{3,2},{4,5},{5,4},{6,7},{7,6},{8,9},{9,8},{10,11... | collective-permute-start | bytes 2359304 | tf_op jit(solution)/shard_map/ppermute | solution.py:131
Sparse Core Ops, SparseCore 0:
  10.3 45.2 all-gather.3
  57.9 44.2 all-gather.5
  104.5 44.0 all-gather.7
where the time goes:
time: 231 us
  Pallas kernels  80 us (35%)
  local copies, waits for them, and re-layouts  44.4 us (19%)
  waiting for transfers between devices  43.8 us (19%)
  other arithmetic  21 us (9%)
  matrix products  20.5 us (9%)
  between operations  16.2 us (7%)
  starting transfers between devices  4.71 us (2%)
    pallas_call x1, Pallas kernels, flash_attend(): pl.pallas_call(kernel, grid_spec=grid_spec, out_shape=jax.ShapeDtypeStruc...  80 us
    ppermute x4, waiting for transfers between devices, shifted(): lax.ppermute(values, 'ep', [(i, (i + shift) % devices) for i in range(dev...  42.3 us
    unnamed x45, local copies, waits for them, and re-layouts  18.6 us
    dynamic_update_slice x1, local copies, waits for them, and re-layouts, on_device(): keys = lax.dynamic_update_slice(key_cache[0], key_new, (zero, length, zero))  4.98 us
    dynamic_update_slice x1, local copies, waits for them, and re-layouts, on_device(): lax.dynamic_update_slice(value_cache[0], value_new, (zero, length, zero))  4.94 us
    another operation x2, local copies, waits for them, and re-layouts  4.78 us
    dot_general x1, matrix products, on_device(): jnp.einsum('ect,ecd->td', table, contrib, preferred_element_type=jnp.floa...  4.78 us
  transfers between devices with their start and end apart: 7, of which 3 were waited for; matrix products, arithmetic and copies ran while one was open for 30% of the time, Pallas kernels for 35%

commit v1 on v0

--- a/solution.py
+++ b/solution.py
@@ -38,81 +38,84 @@
     return (table.astype(jnp.bfloat16), gate_slot)
 
 
-def flash_attend(query, keys, values, length, new_rows):
+def flash_attend(query, keys, values, key_new, value_new, length):
     kv_heads, rows, head_dim = query.shape
-    block = new_rows
-    blocks = keys.shape[1] // block
-    limit = (length + jnp.arange(rows, dtype=jnp.int32) % new_rows)[:, None]
-
-    def last_block(length_ref):
-        return (length_ref[0] + new_rows - 1) // block
-
-    def kernel(length_ref, limit_ref, q_ref, k_ref, v_ref, o_ref, m_sc, l_sc, acc_sc):
+    block = key_new.shape[2]
+    blocks = keys.shape[2] // block
+
+    def cached_blocks(length_ref):
+        return (length_ref[0] + block - 1) // block
+
+    def kernel(length_ref, q_ref, kc_ref, vc_ref, kn_ref, vn_ref, o_ref, m_sc, l_sc, acc_sc):
         step = pl.program_id(1)
-
-        @pl.when(step == 0)
-        def _():
-            m_sc[...] = jnp.full(m_sc.shape, -1e30, jnp.float32)
-            l_sc[...] = jnp.zeros(l_sc.shape, jnp.float32)
-            acc_sc[...] = jnp.zeros(acc_sc.shape, jnp.float32)
-
-        def visit(masked):
-            scores = lax.dot_general(
-                q_ref[0],
-                k_ref[0],
+        length = length_ref[0]
+
+        def visit(key_block, value_block, visible, first):
+            scores = jnp.dot(q_ref[0], key_block, preferred_element_type=jnp.float32)
+            scores = jnp.where(visible, scores, -1e30)
+            if first:
+                highest = jnp.max(scores, -1, keepdims=True)
+            else:
+                previous = m_sc[...]
+                highest = jnp.maximum(previous, jnp.max(scores, -1, keepdims=True))
+            probs = jnp.where(visible, jnp.exp(scores - highest), 0.0)
+            summed = lax.dot_general(
+                probs.astype(jnp.bfloat16),
+                value_block,
                 (((1,), (1,)), ((), ())),
                 preferred_element_type=jnp.float32,
             )
-            if masked:
-                column = step * block + lax.broadcasted_iota(jnp.int32, scores.shape, 1)
-                visible = column <= limit_ref[...]
-                scores = jnp.where(visible, scores, -1e30)
-            previous = m_sc[...]
-            highest = jnp.maximum(previous, jnp.max(scores, -1, keepdims=True))
-            probs = jnp.exp(scores - highest)
-            if masked:
-                probs = jnp.where(visible, probs, 0.0)
-            correction = jnp.exp(previous - highest)
-            l_sc[...] = l_sc[...] * correction + jnp.sum(probs, -1, keepdims=True)
-            acc_sc[...] = acc_sc[...] * correction + jnp.dot(
-                probs.astype(jnp.bfloat16), v_ref[0], preferred_element_type=jnp.float32
-            )
+            if first:
+                l_sc[...] = jnp.sum(probs, -1, keepdims=True)
+                acc_sc[...] = summed
+            else:
+                correction = jnp.exp(previous - highest)
+                l_sc[...] = l_sc[...] * correction + jnp.sum(probs, -1, keepdims=True)
+                acc_sc[...] = acc_sc[...] * correction + summed
             m_sc[...] = highest
 
-        whole = (step + 1) * block - 1 <= length_ref[0]
-
-        @pl.when(whole)
+        shape = (rows, block)
+        column = lax.broadcasted_iota(jnp.int32, shape, 1)
+
+        @pl.when(step == 0)
         def _():
-            visit(False)
-
-        @pl.when(jnp.logical_not(whole) & (step <= last_block(length_ref)))
+            token = lax.rem(lax.broadcasted_iota(jnp.int32, shape, 0), block)
+            visit(kn_ref[0], vn_ref[0], column <= token, True)
+
+        start = (step - 1) * block
+
+        @pl.when((step > 0) & (start < length))
         def _():
-            visit(True)
+            visit(kc_ref[0], vc_ref[0], column + start < length, False)
 
         @pl.when(step == blocks - 1)
         def _():
             o_ref[0] = (acc_sc[...] / l_sc[...]).astype(o_ref.dtype)
 
-    def kv_map(head, step, length_ref):
-        return (head, jnp.minimum(step, last_block(length_ref)), 0)
+    def cache_map(head, step, length_ref):
+        return (head, 0, jnp.clip(step - 1, 0, cached_blocks(length_ref) - 1))
+
+    def fixed_map(head, step, length_ref):
+        return (head, 0, 0)
 
     grid_spec = pltpu.PrefetchScalarGridSpec(
         num_scalar_prefetch=1,
         grid=(kv_heads, blocks),
         in_specs=[
-            pl.BlockSpec((rows, 1), lambda head, step, length_ref: (0, 0)),
-            pl.BlockSpec((1, rows, head_dim), lambda head, step, length_ref: (head, 0, 0)),
-            pl.BlockSpec((1, block, head_dim), kv_map),
-            pl.BlockSpec((1, block, head_dim), kv_map),
+            pl.BlockSpec((1, rows, head_dim), fixed_map),
+            pl.BlockSpec((1, head_dim, block), cache_map),
+            pl.BlockSpec((1, head_dim, block), cache_map),
+            pl.BlockSpec((1, head_dim, block), fixed_map),
+            pl.BlockSpec((1, head_dim, block), fixed_map),
         ],
-        out_specs=pl.BlockSpec((1, rows, head_dim), lambda head, step, length_ref: (head, 0, 0)),
+        out_specs=pl.BlockSpec((1, rows, head_dim), fixed_map),
         scratch_shapes=[
             pltpu.VMEM((rows, 1), jnp.float32),
             pltpu.VMEM((rows, 1), jnp.float32),
             pltpu.VMEM((rows, head_dim), jnp.float32),
         ],
     )
-    flops = 4 * kv_heads * rows * keys.shape[1] * head_dim
+    flops = 4 * kv_heads * rows * keys.shape[2] * head_dim
     return pl.pallas_call(
         kernel,
         grid_spec=grid_spec,
@@ -120,10 +123,10 @@
         compiler_params=pltpu.CompilerParams(dimension_semantics=("arbitrary", "arbitrary")),
         cost_estimate=pl.CostEstimate(
             flops=flops,
-            transcendentals=kv_heads * rows * keys.shape[1],
+            transcendentals=kv_heads * rows * keys.shape[2],
             bytes_accessed=2 * (query.size + keys.size + values.size + query.size),
         ),
-    )(length.reshape(1), limit, query, keys, values)
+    )(length.reshape(1), query, keys, values, key_new, value_new)
 
 
 def shifted(values, shift):
@@ -219,7 +222,14 @@
     zero = jnp.zeros((), jnp.int32)
     keys = lax.dynamic_update_slice(key_cache[0], key_new, (zero, length, zero))
     values = lax.dynamic_update_slice(value_cache[0], value_new, (zero, length, zero))
-    attended = flash_attend(query, keys, values, length, new_rows)
+    attended = flash_attend(
+        query,
+        jnp.swapaxes(key_cache[0], 1, 2),
+        jnp.swapaxes(value_cache[0], 1, 2),
+        jnp.swapaxes(key_new, 1, 2),
+        jnp.swapaxes(value_new, 1, 2),
+        length,
+    )
     attended = (
         attended.reshape(heads_local, new_rows, head_dim)
         .transpose(1, 0, 2)

time: 231 us -> 200 us (0.87)
  the two profiles are of different devices: /device:TPU:18 before, /device:TPU:8 now
where the time goes in v1:
time: 200 us; the launch traced here: 199 us
  Pallas kernels  70.1 us (35%)
  waiting for transfers between devices  55.5 us (28%)
  local copies, waits for them, and re-layouts  21.1 us (11%)
  matrix products  17.4 us (9%)
  between operations  16 us (8%)
  other arithmetic  13.7 us (7%)
  starting transfers between devices  5.23 us (3%)
    pallas_call x1, Pallas kernels, flash_attend(): pl.pallas_call(kernel, grid_spec=grid_spec, out_shape=jax.ShapeDtypeStruc...  70.1 us
    ppermute x4, waiting for transfers between devices, shifted(): lax.ppermute(values, 'ep', [(i, (i + shift) % devices) for i in range(dev...  54.7 us
    unnamed x49, local copies, waits for them, and re-layouts  5.67 us
    ppermute x4, starting transfers between devices, shifted(): lax.ppermute(values, 'ep', [(i, (i + shift) % devices) for i in range(dev...  5.12 us
    dot_general x1, matrix products, on_device(): jnp.einsum('ect,ecd->td', table, contrib, preferred_element_type=jnp.floa...  4.78 us
  transfers between devices with their start and end apart: 7, of which 4 were waited for; matrix products, arithmetic and copies ran while one was open for 16% of the time, Pallas kernels for 35%

profile of v1, /device:TPU:8, one launch (start us, length us, event | category | flops | bytes accessed | tf_op | source)
XLA Modules:
  0.0 199.2 jit_solution(82247638022343795)
XLA Ops:
  7.2 0.0 copy-start
  7.2 0.0 all-gather.4.cloned.1.call-start
  7.2 2.6 %copy.45 = bf16[1,4,2560,64]{2,3,1,0:T(8,128)(2,1)} copy(bf16[1,4,2560,64]{2,3,1,0:T(8,128)(2,1)} %param.18) | data formatting | bytes 2621440
  9.9 0.0 copy-start.22
  9.9 1.1 copy.44
  10.9 0.0 all-gather.4.cloned.1.call-update
  11.0 0.0 all-gather.6.cloned.1.call-start
  11.0 0.7 all-gather.6.cloned.1.call-update
  11.7 0.0 all-gather.8.cloned.1.call-start
  11.8 1.6 collective-permute-start
  13.4 0.0 all-gather.8.cloned.1.call-update
  13.5 0.1 fusion.20
  13.6 0.6 reduce-window.6
  14.2 0.6 fusion.22
  14.8 1.3 fusion.23
  16.2 0.6 add_convert_fusion.3
  16.8 0.3 multiply_cosine_fusion
  17.1 0.1 broadcast_in_dim.33
  17.2 0.1 constant_dynamic-update-slice_fusion.1
  17.3 0.0 copy-start.18
  17.3 13.9 %collective-permute-done = bf16[512,768]{1,0:T(8,128)(2,1)} collective-permute-done((bf16[512,768]{1,0:T(8,128)(2,1)S(1)}, bf16[512,768]{1,0:T(8,128)(2,1)}, u32[]{:S(2)}, u32[]{:S(2)}) %collective-permute-start) | collective-permute-done | bytes 786464 | tf_op jit(solution)/shard_map/ppermute | solution.py:134
  31.2 1.2 constant_dynamic-update-slice_fusion
  32.4 0.4 fusion
  32.8 1.6 fusion.27
  34.4 0.3 subtract_convert_fusion
  34.7 1.5 copy.31
  36.2 1.5 copy.32
  37.7 2.9 %fusion.25 = f32[512,256]{0,1:T(8,128)S(1)} fusion(bf16[1536,256]{1,0:T(8,128)(2,1)} %param.26, bf16[512,1536]{1,0:T(8,128)(2,1)} %copy-done.2, f32[1536]{0:T(1024)S(1)} %copy-done.20, f32[512]{0:T(512)S(1)} %add_rsqrt_fusion.1), kind=kOutput, calls=%fused_computation.60 | convolution fusion | flops 405798912 | bytes 2891776 | tf_op jit(solution)/shard_map/dot_general | solution.py:209
  40.6 0.1 subtract_convert_fusion.1
  40.7 0.8 maximum_bitcast_fusion.kn_ref
  41.5 0.0 copy-start.19
  41.5 2.1 %maximum_multiply_fusion.q_ref = bf16[4,1536,64]{2,1,0:T(8,128)(2,1)} fusion(bf16[4,1536,32]{2,1,0:T(8,128)(2,1)S(1)} %bitcast.64, bf16[4,1536,32]{2,1,0:T(8,128)(2,1)S(1)} %bitcast.63), kind=kLoop, calls=%fused_computation.17 | loop fusion | flops 2359296 | bytes 1572864 | tf_op jit(solution)/shard_map/mul | solution.py:212
  43.7 1.5 convolution_convert_fusion.2
  45.2 70.1 %shard_map.175 = bf16[4,1536,64]{2,1,0:T(8,128)(2,1)} custom-call(s32[1]{0:T(128)} %bitcast.1.length_ref, bf16[4,1536,64]{2,1,0:T(8,128)(2,1)} %maximum_multiply_fusion.q_ref, bf16[4,64,2560]{2,1,0:T(8,128)(2,1)} %bitcast.69, bf16[4,64,2560]{2,1,0:T(8,128)(2,1)} %bitcast.68, bf16[4,64,512]{2,1,0:T(8,128)(2,1)} %maximum_bitcast_fusion.kn_ref, ...), custom_call_target="tpu_custom_call" | custom-call | flops 4026531840 | bytes 4194304 | tf_op jit(solution)/shard_map/pallas_call | solution.py:119
  115.3 1.9 copy.33
  117.2 1.4 convolution_convert_fusion
  118.6 0.0 copy-start.15
  118.6 1.4 fusion.30
  120.0 0.2 copy-done.4
  120.2 1.5 collective-permute-start.1
  121.7 0.5 collective-permute-start.2
  122.2 0.2 slice_reduce_fusion
  122.4 0.2 reduce-window.9
  122.6 0.1 add_bitcast_fusion
  122.7 0.1 fusion.21
  122.8 0.2 select_reduce_fusion
  123.1 17.8 %collective-permute-done.1 = bf16[256,1536]{1,0:T(8,128)(2,1)S(1)} collective-permute-done((bf16[256,1536]{1,0:T(8,128)(2,1)}, bf16[256,1536]{1,0:T(8,128)(2,1)S(1)}, u32[]{:S(2)}, u32[]{:S(2)}) %collective-permute-start.1) | collective-permute-done | bytes 786464 | tf_op jit(solution)/shard_map/ppermute | solution.py:134
  140.9 14.5 %collective-permute-done.2 = bf16[256,1536]{1,0:T(8,128)(2,1)} collective-permute-done((bf16[256,1536]{1,0:T(8,128)(2,1)}, bf16[256,1536]{1,0:T(8,128)(2,1)}, u32[]{:S(2)}, u32[]{:S(2)}) %collective-permute-start.2) | collective-permute-done | bytes 786464 | tf_op jit(solution)/shard_map/ppermute | solution.py:134
  155.4 2.9 %multiply_reduce_fusion = (f32[512]{0:T(512)S(1)}, f32[512,1536]{1,0:T(8,128)S(1)}) fusion(bf16[256,1536]{1,0:T(8,128)(2,1)} %collective-permute-done.2, bf16[256,1536]{1,0:T(8,128)(2,1)S(1)} %collective-permute-done.1, bf16[512,1536]{1,0:T(8,128)(2,1)} %copy-done.4, bf16[512,1536]{1,0:T(8,128)(2,1)} %copy-done.2), kind=kLoop, calls=%fused_computation.9 | loop fusion | flops 9436672 | bytes 7866368 | tf_op jit(solution)/shard_map/reduce_sum | solution.py:12
  158.3 1.6 copy-done.1
  160.0 0.9 convolution_convert_fusion.1
  160.9 0.0 all-gather.4.cloned.1.call-done
  160.9 0.0 all-gather.6.cloned.1.call-done
  161.0 0.0 all-gather.8.cloned.1.call-done
  161.0 2.8 %fusion.31 = f32[2,192,512]{2,1,0:T(8,128)S(1)} fusion(bf16[2,192,1536]{2,1,0:T(8,128)(2,1)S(1)} %convolution_convert_fusion.1, bf16[2,1536,512]{2,1,0:T(8,128)(2,1)} %all-gather.4.cloned.1.call-done), kind=kOutput, calls=%fused_computation.63 | convolution fusion | flops 603979776 | bytes 5111808 | tf_op jit(solution)/shard_map/ecd,edf->ecf/dot_general | solution.py:254
  163.8 0.0 copy-done.17
  163.8 1.6 fusion.11
  165.4 4.8 %fusion.4 = bf16[512,1536]{1,0:T(8,128)(2,1)} fusion(bf16[2,192,512]{2,1,0:T(8,128)(2,1)} %fusion.11, bf16[2,512,1536]{2,1,0:T(8,128)(2,1)} %all-gather.8.cloned.1.call-done, f32[2,192]{1,0:T(2,128)S(1)} %select_reduce_fusion, s32[2,512]{1,0:T(2,128)S(1)} %bitcast.81, pred[2,512]{1,0:T(4,128)(4,1)S(1)} %broadcast_compare_fusion), kind=kOutput, calls=%fused_computation.11 | convolution fusion | flops 1210318848 | bytes 5118464 | tf_op jit(solution)/shard_map/ect,ecd->td/dot_general | solution.py:259
  170.2 2.1 %constant_dynamic-slice_fusion = bf16[512,768]{1,0:T(8,128)(2,1)} fusion(bf16[512,1536]{1,0:T(8,128)(2,1)} %fusion.4, s32[]{:T(128)S(6)} %select_n.57), kind=kLoop, calls=%fused_computation.53 | loop fusion | bytes 1572868 | tf_op jit(solution)/shard_map/dynamic_slice | solution.py:166
  172.3 1.5 collective-permute-start.3
  175.7 2.8 %dynamic_update_slice.16 = bf16[1,4,2560,64]{2,3,1,0:T(8,128)(2,1)} dynamic-update-slice(bf16[1,4,2560,64]{2,3,1,0:T(8,128)(2,1)} %copy.44, bf16[1,4,512,64]{2,3,1,0:T(8,128)(2,1)S(1)} %pad_maximum_fusion, s32[]{:T(128)} %constant.50.clone.1, s32[]{:T(128)} %constant.50.clone.1, s32[]{:T(128)S(6)} %select_n.58, s32[]{:T(128)} %constant.50.clone.1) | dynamic-update-slice | bytes 524292 | tf_op jit(solution)/shard_map/dynamic_update_slice | solution.py:223
  178.5 2.7 %dynamic_update_slice.17 = bf16[1,4,2560,64]{2,3,1,0:T(8,128)(2,1)} dynamic-update-slice(bf16[1,4,2560,64]{2,3,1,0:T(8,128)(2,1)} %copy.45, bf16[1,4,512,64]{2,3,1,0:T(8,128)(2,1)S(1)} %bitcast.75, s32[]{:T(128)} %constant.50.clone.1, s32[]{:T(128)} %constant.50.clone.1, s32[]{:T(128)S(6)} %select_n.58, s32[]{:T(128)} %constant.50.clone.1) | dynamic-update-slice | bytes 524292 | tf_op jit(solution)/shard_map/dynamic_update_slice | solution.py:224
  181.2 8.5 %collective-permute-done.3 = bf16[512,768]{1,0:T(8,128)(2,1)} collective-permute-done((bf16[512,768]{1,0:T(8,128)(2,1)}, bf16[512,768]{1,0:T(8,128)(2,1)}, u32[]{:S(2)}, u32[]{:S(2)}) %collective-permute-start.3) | collective-permute-done | bytes 786464 | tf_op jit(solution)/shard_map/ppermute | solution.py:134
  189.7 3.0 %fusion.12 = bf16[1,512,768]{2,1,0:T(8,128)(2,1)} fusion(bf16[512,768]{1,0:T(8,128)(2,1)} %collective-permute-done.3, f32[512,1536]{1,0:T(8,128)} %copy-done.1, s32[]{:T(128)S(6)} %select_n.53, bf16[512,1536]{1,0:T(8,128)(2,1)} %fusion.4), kind=kLoop, calls=%fused_computation.24 | loop fusion | flops 1966080 | bytes 3932164 | tf_op jit(solution)/shard_map/broadcast_in_dim | solution.py:265
  (46 shorter events, 0.2 us)
Async XLA Ops:
  7.2 110.0 %copy-start = (bf16[768,1536]{1,0:T(8,128)(2,1)S(1)}, bf16[768,1536]{1,0:T(8,128)(2,1)}, u32[]{:S(2)}) copy-start(bf16[768,1536]{1,0:T(8,128)(2,1)} %param.28) | copy-start | bytes 7077892
  7.2 153.8 %all-gather.4.cloned.1.call-start = ((), (), s32[]{:S(2)}) async-start(), calls=%async_computation | async-start | bytes 3342336 | tf_op jit(solution)/shard_map/all_gather | solution.py:199
  7.2 2.6 %copy-start.7 = (bf16[1,4,2560,64]{2,3,1,0:T(8,128)(2,1)S(1)}, bf16[1,4,2560,64]{2,3,1,0:T(8,128)(2,1)}, u32[]{:S(2)}) copy-start(bf16[1,4,2560,64]{2,3,1,0:T(8,128)(2,1)} %param.17) | copy-start | bytes 3932164
  9.9 1.9 copy-start.12
  9.9 3.6 %copy-start.14 = (s32[1,512,8]{1,2,0:T(8,128)S(1)}, s32[1,512,8]{1,2,0:T(8,128)}, u32[]{:S(2)}) copy-start(s32[1,512,8]{1,2,0:T(8,128)} %param.21) | copy-start | bytes 49156
  9.9 4.3 %copy-start.21 = (s32[16]{0:T(128)S(1)}, s32[16]{0:T(128)}, u32[]{:S(2)}) copy-start(s32[16]{0:T(128)} %param.19) | copy-start | bytes 196
  9.9 5.0 %copy-start.22 = (s32[16]{0:T(128)S(1)}, s32[16]{0:T(128)}, u32[]{:S(2)}) copy-start(s32[16]{0:T(128)} %param.20) | copy-start | bytes 196
  11.0 150.0 %all-gather.6.cloned.1.call-start = ((), (), s32[]{:S(2)}) async-start(), calls=%async_computation.1 | async-start | bytes 3342336 | tf_op jit(solution)/shard_map/all_gather | solution.py:200
  11.7 149.3 %all-gather.8.cloned.1.call-start = ((), (), s32[]{:S(2)}) async-start(), calls=%async_computation.2 | async-start | bytes 3342336 | tf_op jit(solution)/shard_map/all_gather | solution.py:201
  11.8 19.5 %collective-permute-start = (bf16[512,768]{1,0:T(8,128)(2,1)S(1)}, bf16[512,768]{1,0:T(8,128)(2,1)}, u32[]{:S(2)}, u32[]{:S(2)}) collective-permute-start(bf16[512,768]{1,0:T(8,128)(2,1)S(1)} %bitcast.72), channel_id=1, source_target_pairs={{0,1},{1,0},{2,3},{3,2},{4,5},{5,4},{6,7},{7,6},{8,9},{9,8},{10,11... | collective-permute-start | bytes 2359304 | tf_op jit(solution)/shard_map/ppermute | solution.py:134
  17.3 15.5 %copy-start.18 = (bf16[1536,768]{1,0:T(8,128)(2,1)S(1)}, bf16[1536,768]{1,0:T(8,128)(2,1)}, u32[]{:S(2)}) copy-start(bf16[1536,768]{1,0:T(8,128)(2,1)} %param.25) | copy-start | bytes 7077892
  17.3 15.5 %copy-start.20 = (f32[1536]{0:T(1024)S(1)}, f32[1536]{0:T(1024)}, u32[]{:S(2)}) copy-start(f32[1536]{0:T(1024)} %param.23) | copy-start | bytes 18436
  32.4 2.0 copy-start.2
  37.7 3.8 %copy-start.5 = (bf16[12,512,32]{2,1,0:T(8,128)(2,1)S(1)}, bf16[12,512,32]{2,1,0:T(8,128)(2,1)}, u32[]{:S(2)}) copy-start(bf16[12,512,32]{2,1,0:T(8,128)(2,1)} %copy.31) | copy-start | bytes 1179652
  37.7 3.8 %copy-start.6 = (bf16[12,512,32]{2,1,0:T(8,128)(2,1)S(1)}, bf16[12,512,32]{2,1,0:T(8,128)(2,1)}, u32[]{:S(2)}) copy-start(bf16[12,512,32]{2,1,0:T(8,128)(2,1)} %copy.32) | copy-start | bytes 1179652
  40.7 0.8 copy-start.8
  40.7 0.8 copy-start.10
  41.5 2.2 %copy-start.3 = (bf16[512,1536]{1,0:T(8,128)(2,1)S(1)}, bf16[512,1536]{1,0:T(8,128)(2,1)}, u32[]{:S(2)}) copy-start(bf16[512,1536]{1,0:T(8,128)(2,1)} %copy-done.2) | copy-start | bytes 4718596
  41.5 2.1 %copy-start.19 = (bf16[1536,256]{1,0:T(8,128)(2,1)S(1)}, bf16[1536,256]{1,0:T(8,128)(2,1)}, u32[]{:S(2)}) copy-start(bf16[1536,256]{1,0:T(8,128)(2,1)} %param.27) | copy-start | bytes 2359300
  118.6 1.6 copy-start.4
  118.6 4.1 %copy-start.15 = (f32[1,512,8]{1,2,0:T(8,128)S(1)}, f32[1,512,8]{1,2,0:T(8,128)}, u32[]{:S(2)}) copy-start(f32[1,512,8]{1,2,0:T(8,128)} %param.22) | copy-start | bytes 49156
  120.2 20.7 %collective-permute-start.1 = (bf16[256,1536]{1,0:T(8,128)(2,1)}, bf16[256,1536]{1,0:T(8,128)(2,1)S(1)}, u32[]{:S(2)}, u32[]{:S(2)}) collective-permute-start(bf16[256,1536]{1,0:T(8,128)(2,1)} %get-tuple-element.15), channel_id=1, source_target_pairs={{0,1},{1,0},{2,3},{3,2},{4,5},{5,4},{6,7},{7,6},{8,9},{9,8},{10,11... | collective-permute-start | bytes 2359304 | tf_op jit(solution)/shard_map/ppermute | solution.py:134
  121.7 33.7 %collective-permute-start.2 = (bf16[256,1536]{1,0:T(8,128)(2,1)}, bf16[256,1536]{1,0:T(8,128)(2,1)}, u32[]{:S(2)}, u32[]{:S(2)}) collective-permute-start(bf16[256,1536]{1,0:T(8,128)(2,1)} %get-tuple-element.16), channel_id=1, source_target_pairs={{0,1},{1,0},{2,3},{3,2},{4,5},{5,4},{6,7},{7,6},{8,9},{9,8},{10,11... | collective-permute-start | bytes 2359304 | tf_op jit(solution)/shard_map/ppermute | solution.py:134
  123.1 36.9 %copy-start.16 = (f32[1536]{0:T(1024)S(1)}, f32[1536]{0:T(1024)}, u32[]{:S(2)}) copy-start(f32[1536]{0:T(1024)} %param.24) | copy-start | bytes 18436
  158.3 1.7 copy-start.1
  161.0 2.8 %copy-start.17 = (bf16[2,1536,512]{2,1,0:T(8,128)(2,1)S(1)}, bf16[2,1536,512]{2,1,0:T(8,128)(2,1)}, u32[]{:S(2)}) copy-start(bf16[2,1536,512]{2,1,0:T(8,128)(2,1)} %all-gather.6.cloned.1.call-done) | copy-start | bytes 9437188
  170.2 5.5 %copy-start.9 = (bf16[4,512,32]{1,2,0:T(8,128)(2,1)S(1)}, bf16[4,512,32]{1,2,0:T(8,128)(2,1)}, u32[]{:S(2)}) copy-start(bf16[4,512,32]{1,2,0:T(8,128)(2,1)} %copy-done.8) | copy-start | bytes 393220
  170.2 5.5 %copy-start.11 = (bf16[4,512,32]{1,2,0:T(8,128)(2,1)S(1)}, bf16[4,512,32]{1,2,0:T(8,128)(2,1)}, u32[]{:S(2)}) copy-start(bf16[4,512,32]{1,2,0:T(8,128)(2,1)} %copy-done.10) | copy-start | bytes 393220
  170.2 8.3 %copy-start.13 = (bf16[512,256]{0,1:T(8,128)(2,1)S(1)}, bf16[512,256]{0,1:T(8,128)(2,1)}, u32[]{:S(2)}) copy-start(bf16[512,256]{0,1:T(8,128)(2,1)} %convolution_convert_fusion.2) | copy-start | bytes 786436
  172.3 17.5 %collective-permute-start.3 = (bf16[512,768]{1,0:T(8,128)(2,1)}, bf16[512,768]{1,0:T(8,128)(2,1)}, u32[]{:S(2)}, u32[]{:S(2)}) collective-permute-start(bf16[512,768]{1,0:T(8,128)(2,1)} %constant_dynamic-slice_fusion), channel_id=1, source_target_pairs={{0,1},{1,0},{2,3},{3,2},{4,5},{5,4},{6,7},{7,6},{8,9},{9,8},{10,11... | collective-permute-start | bytes 2359304 | tf_op jit(solution)/shard_map/ppermute | solution.py:134
Sparse Core Ops, SparseCore 0:
  11.1 46.9 all-gather.3
  60.4 44.0 all-gather.5
  106.8 44.0 all-gather.7
